TPU v7x, 512 devices: a whole 4x4x16 slice. The times are simulated.
512 devices in a mesh: patch: 128 (over z, y, core), mp: 4 (over x).
Axes of the slice: x: 4, y: 4, z: 16, core: 2. Of those that a mesh axis runs over, the one named last changes fastest.
Arguments:
- features: bfloat16 [65536, 1024], P('patch'), may hold values from -16 to 16
- gain_attn: float32 [1024], replicated, may hold values from 0.1 to 1.9
- w_qkv: bfloat16 [3, 1024, 1024], P(None, None, 'mp'), as said below
- w_out: bfloat16 [1024, 1024], P('mp'), may hold values from -0.1875 to 0.1875
- gain_mlp: float32 [1024], replicated, may hold values from 0.1 to 1.9
- w_up: bfloat16 [1024, 2048], P(None, 'mp'), may hold values from -0.1875 to 0.1875
- w_down: bfloat16 [2048, 1024], P('mp'), may hold values from -0.125 to 0.125
- neighbours: int32 [512, 8], replicated, may hold values from 0 to 511, as said below
Outputs:
- layer_out: bfloat16 [65536, 1024], P('patch', 'mp')
Inputs may be any that keep to these rules, and one draw needn't show every extreme that they name: `neighbours`: row p lists 8 different patches; the first is p itself. Patch q belongs to device q // 4 of the patch axis, and every listed patch belongs to a device whose index differs from that of p's device by at most 2 around the patch axis (the lining closes into a cycle). `w_qkv`: projection weights of mean zero.
All inputs are finite; a program needn't handle non-finite values.
Results may differ from a plain program's by a relative error of at most 0.012.
Values may be sent and summed in bfloat16 or wider, within the bound.
No kernel may reach another device: no remote copies, remote signals or barrier semaphores. Data moves between devices by JAX's collectives and lax.ppermute only.
A program may use at most 64 MiB of HBM per device.

v0:
```python
import jax
import jax.numpy as jnp
from jax import lax
from jax.sharding import PartitionSpec as P

D = 1024
HD = 64
PN = 128
K_NB = 8
REACH = 2


def from_behind(array, axis, by):
    length = lax.axis_size(axis)
    return lax.ppermute(array, axis, [(i, (i + by) % length) for i in range(length)])


def normalize(rows, gain):
    rows32 = rows.astype(jnp.float32)
    mean_sq = jnp.mean(rows32 * rows32, axis=-1, keepdims=True)
    return (rows32 * lax.rsqrt(mean_sq + 1e-05) * gain).astype(jnp.bfloat16)


def per_device(features, gain_attn, w_qkv, w_out, gain_mlp, w_up, w_down, neighbours):
    row_count = features.shape[0]
    patches_here = row_count // PN
    heads_here = w_qkv.shape[2] // HD
    normed = normalize(features, gain_attn)
    queries = jnp.dot(normed, w_qkv[0], preferred_element_type=jnp.float32).astype(jnp.bfloat16)
    own_keys = (
        jnp.dot(normed, w_qkv[1], preferred_element_type=jnp.float32)
        .astype(jnp.bfloat16)
        .reshape(patches_here, PN, -1)
    )
    own_vals = (
        jnp.dot(normed, w_qkv[2], preferred_element_type=jnp.float32)
        .astype(jnp.bfloat16)
        .reshape(patches_here, PN, -1)
    )
    window = {0: (own_keys, own_vals)}
    for offset in range(-REACH, REACH + 1):
        if offset != 0:
            window[offset] = from_behind((own_keys, own_vals), "patch", -offset)
    keys_win = jnp.concatenate([window[offset][0] for offset in range(-REACH, REACH + 1)], axis=0)
    vals_win = jnp.concatenate([window[offset][1] for offset in range(-REACH, REACH + 1)], axis=0)
    device = lax.axis_index("patch")
    n_dev = lax.axis_size("patch")
    listed = lax.dynamic_slice_in_dim(neighbours, device * patches_here, patches_here, 0)
    owner_dev = listed // patches_here
    offset_dev = jnp.mod(owner_dev - device + n_dev // 2, n_dev) - n_dev // 2
    slot_index = (offset_dev + REACH) * patches_here + jnp.mod(listed, patches_here)
    keys_nb = keys_win[slot_index].reshape(patches_here, K_NB * PN, heads_here, HD)
    vals_nb = vals_win[slot_index].reshape(patches_here, K_NB * PN, heads_here, HD)
    query_blk = queries.reshape(patches_here, PN, heads_here, HD)
    scores = jnp.einsum(
        "pqhd,pkhd->phqk", query_blk, keys_nb, preferred_element_type=jnp.float32
    ) * (1.0 / HD**0.5)
    probs = jax.nn.softmax(scores, axis=-1).astype(jnp.bfloat16)
    mixed_rows = jnp.einsum("phqk,pkhd->pqhd", probs, vals_nb, preferred_element_type=jnp.float32)
    attended = mixed_rows.astype(jnp.bfloat16).reshape(row_count, heads_here * HD)
    partial_value = jnp.dot(attended, w_out, preferred_element_type=jnp.float32)
    col_share = lax.psum_scatter(
        partial_value.astype(jnp.bfloat16), "mp", scatter_dimension=1, tiled=True
    ).astype(jnp.float32)
    col_width = col_share.shape[1]
    col_begin = lax.axis_index("mp") * col_width
    residual_cols = (
        lax.dynamic_slice_in_dim(features, col_begin, col_width, 1).astype(jnp.float32) + col_share
    )
    gain_cols = lax.dynamic_slice_in_dim(gain_mlp, col_begin, col_width, 0)
    square_sum = lax.psum(jnp.sum(residual_cols * residual_cols, axis=1), "mp")
    inverse_rms = lax.rsqrt(square_sum / D + 1e-05)
    normed_cols = (residual_cols * inverse_rms[:, None] * gain_cols).astype(jnp.bfloat16)
    normed2 = lax.all_gather(normed_cols, "mp", axis=1, tiled=True)
    hidden = jax.nn.gelu(
        jnp.dot(normed2, w_up, preferred_element_type=jnp.float32), approximate=True
    ).astype(jnp.bfloat16)
    down_term = jnp.dot(hidden, w_down, preferred_element_type=jnp.float32)
    down_cols = lax.psum_scatter(
        down_term.astype(jnp.bfloat16), "mp", scatter_dimension=1, tiled=True
    ).astype(jnp.float32)
    return (residual_cols + down_cols).astype(jnp.bfloat16)


def solution(mesh):
    return jax.shard_map(
        per_device,
        mesh=mesh,
        in_specs=(
            P("patch", None),
            P(),
            P(None, None, "mp"),
            P("mp", None),
            P(),
            P(None, "mp"),
            P("mp", None),
            P(),
        ),
        out_specs=P("patch", "mp"),
        check_vma=False,
    )
```

profile of v0, /device:TPU:8, one launch (start us, length us, event | category | flops | bytes accessed | tf_op | source)
XLA Modules:
  0.0 209.8 jit_solution(8594160232992480794)
XLA Ops:
  6.5 0.0 copy-start.6
  6.6 1.7 fusion.9
  8.2 1.9 convolution_convert_fusion.2
  10.1 3.5 %collective-permute-start.4 = (bf16[4,128,256]{2,1,0:T(8,128)(2,1)S(1)}, bf16[4,128,256]{2,1,0:T(8,128)(2,1)}, u32[]{:S(2)}, u32[]{:S(2)}) collective-permute-start(bf16[4,128,256]{2,1,0:T(8,128)(2,1)S(1)} %bitcast.30), channel_id=1, source_target_pairs={{0,8},{4,12},{8,16},{12,20},{16,24},{20,28},{24,32},{28,36},{32,40... | collective-permute-start | bytes 786440 | tf_op jit(solution)/shard_map/ppermute | solution.py:15
  13.6 1.9 collective-permute-start.5
  15.5 3.6 %collective-permute-start.6 = (bf16[4,128,256]{2,1,0:T(8,128)(2,1)S(1)}, bf16[4,128,256]{2,1,0:T(8,128)(2,1)S(1)}, u32[]{:S(2)}, u32[]{:S(2)}) collective-permute-start(bf16[4,128,256]{2,1,0:T(8,128)(2,1)S(1)} %bitcast.32), channel_id=1, source_target_pairs={{0,508},{4,0},{8,4},{12,8},{16,12},{20,16},{24,20},{28,24},{32,28}... | collective-permute-start | bytes 786440 | tf_op jit(solution)/shard_map/ppermute | solution.py:15
  19.2 10.4 %collective-permute-start.7 = (bf16[4,128,256]{2,1,0:T(8,128)(2,1)S(1)}, bf16[4,128,256]{2,1,0:T(8,128)(2,1)S(1)}, u32[]{:S(2)}, u32[]{:S(2)}) collective-permute-start(bf16[4,128,256]{2,1,0:T(8,128)(2,1)S(1)} %bitcast.33), channel_id=1, source_target_pairs={{0,504},{4,508},{8,0},{12,4},{16,8},{20,12},{24,16},{28,20},{32,24... | collective-permute-start | bytes 786440 | tf_op jit(solution)/shard_map/ppermute | solution.py:15
  29.6 0.0 copy-done.2
  29.6 0.0 copy-done.8
  29.6 0.0 copy-done.6
  29.7 0.5 convolution_convert_fusion.4
  30.1 1.9 collective-permute-start
  32.1 0.5 convolution_convert_fusion.3
  32.6 0.8 compare_select_fusion
  33.4 0.1 copy.17
  33.5 0.1 reshape.39
  33.5 1.0 reshape.60
  34.6 0.0 collective-permute-done.4
  34.6 1.9 collective-permute-start.1
  36.5 1.7 constant_dynamic-update-slice_fusion.9
  38.2 0.0 collective-permute-done.5
  38.2 3.6 %collective-permute-start.2 = (bf16[4,128,256]{2,1,0:T(8,128)(2,1)S(1)}, bf16[4,128,256]{2,1,0:T(8,128)(2,1)}, u32[]{:S(2)}, u32[]{:S(2)}) collective-permute-start(bf16[4,128,256]{2,1,0:T(8,128)(2,1)S(1)} %bitcast.27), channel_id=1, source_target_pairs={{0,508},{4,0},{8,4},{12,8},{16,12},{20,16},{24,20},{28,24},{32,28}... | collective-permute-start | bytes 786440 | tf_op jit(solution)/shard_map/ppermute | solution.py:15
  41.8 1.7 constant_dynamic-update-slice_fusion.8
  43.5 0.7 constant_dynamic-update-slice_fusion.7
  44.2 0.0 collective-permute-done.6
  44.2 7.5 %collective-permute-start.3 = (bf16[4,128,256]{2,1,0:T(8,128)(2,1)S(1)}, bf16[4,128,256]{2,1,0:T(8,128)(2,1)}, u32[]{:S(2)}, u32[]{:S(2)}) collective-permute-start(bf16[4,128,256]{2,1,0:T(8,128)(2,1)S(1)} %bitcast.28), channel_id=1, source_target_pairs={{0,504},{4,508},{8,0},{12,4},{16,8},{20,12},{24,16},{28,20},{32,24... | collective-permute-start | bytes 786440 | tf_op jit(solution)/shard_map/ppermute | solution.py:15
  51.7 0.7 constant_dynamic-update-slice_fusion.6
  52.4 0.0 collective-permute-done.7
  52.5 0.7 constant_dynamic-update-slice_fusion.5
  53.2 2.0 gather_fusion.1
  55.2 3.2 %reshape.61 = bf16[4,1024,4,64]{3,2,1,0:T(4,128)(2,1)} reshape(bf16[32,128,256]{2,1,0:T(8,128)(2,1)S(1)} %gather_fusion.1) | data formatting | bytes 4194304 | tf_op jit(solution)/shard_map/reshape | solution.py:52
  58.4 3.6 %fusion.4 = f32[4,4,128,1024]{3,2,1,0:T(8,128)S(1)} fusion(bf16[4,1024,4,64]{3,2,1,0:T(4,128)(2,1)} %reshape.61, bf16[4,128,4,64]{3,2,1,0:T(4,128)(2,1)} %reshape.60), kind=kOutput, calls=%fused_computation.7 | convolution fusion | flops 268435456 | bytes 10747904 | tf_op jit(solution)/shard_map/pqhd,pkhd->phqk/dot_general | solution.py:55
  62.1 2.2 %fusion.62 = f32[4,4,128]{2,1,0:T(4,128)S(1)} fusion(f32[4,4,128,1024]{3,2,1,0:T(8,128)S(1)} %fusion.4), kind=kOutput, calls=%fused_computation.87 | output fusion | flops 8389631 | bytes 8396800 | tf_op jit(solution)/shard_map/sub | solution.py:58
  64.2 1.0 copy-done.1
  65.3 0.0 collective-permute-done
  65.3 1.7 constant_dynamic-update-slice_fusion.4
  67.0 0.0 collective-permute-done.1
  67.0 1.7 constant_dynamic-update-slice_fusion.3
  68.6 0.7 constant_dynamic-update-slice_fusion.2
  69.4 0.0 collective-permute-done.2
  69.4 1.7 constant_dynamic-update-slice_fusion.1
  71.1 0.0 collective-permute-done.3
  71.1 1.7 constant_dynamic-update-slice_fusion
  72.7 2.0 gather_fusion
  74.7 3.3 %reshape.59 = bf16[4,1024,4,64]{3,2,1,0:T(4,128)(2,1)} reshape(bf16[32,128,256]{2,1,0:T(8,128)(2,1)S(1)} %gather_fusion) | data formatting | bytes 4194304 | tf_op jit(solution)/shard_map/reshape | solution.py:53
  78.0 12.1 %fusion.15 = bf16[4,128,4,64]{1,3,2,0:T(8,128)(2,1)S(1)} fusion(f32[4,4,128]{2,1,0:T(4,128)S(1)} %fusion.62, bf16[4,1024,4,64]{3,2,1,0:T(4,128)(2,1)} %reshape.59, f32[4,4,128,1024]{3,2,1,0:T(8,128)} %copy-done.1), kind=kOutput, calls=%fused_computation.24 | convolution fusion | flops 279055360 | bytes 10756096 | tf_op jit(solution)/shard_map/phqk,pkhd->pqhd/dot_general | solution.py:59
  90.1 0.0 copy-start.3
  90.2 0.2 copy.24
  90.4 1.4 convolution_convert_fusion
  91.8 0.0 reduce-scatter.3.cloned.1.call-update
  91.8 0.0 all-gather.2.cloned.1.call-start
  91.9 0.8 dynamic_slice.11
  92.7 28.3 %reduce-scatter.3.cloned.1.call-done = bf16[512,256]{1,0:T(8,128)(2,1)} async-done(((bf16[512,1024]{1,0:T(8,128)(2,1)}), bf16[512,256]{1,0:T(8,128)(2,1)}) %reduce-scatter.3.cloned.1.call-update) | async-done | bytes 262160 | tf_op jit(solution)/shard_map/reduce_scatter | solution.py:62
  121.1 1.1 multiply_reduce_fusion.1
  122.2 8.4 %psum.7 = f32[512]{0:T(512)S(1)} all-reduce(f32[512]{0:T(512)S(1)} %multiply_reduce_fusion.1), channel_id=1, replica_groups=mesh['patch'=128,'mp'=4] {'mp'}, use_global_device_ids=true, to_apply=%region_5.6 | all-reduce | flops 512 | bytes 4096 | tf_op jit(solution)/shard_map/psum | solution.py:71
  130.6 1.8 multiply_convert_fusion
  132.3 0.0 all-gather.2.cloned.1.call-update
  132.4 0.0 copy-start.4
  132.4 0.0 reduce-scatter.5.cloned.1.call-start
  132.4 32.9 %all-gather.2.cloned.1.call-done = bf16[512,1024]{1,0:T(8,128)(2,1)} async-done(((bf16[512,256]{1,0:T(8,128)(2,1)}), bf16[512,1024]{1,0:T(8,128)(2,1)}) %all-gather.2.cloned.1.call-update) | async-done | bytes 1048592 | tf_op jit(solution)/shard_map/all_gather | solution.py:74
  165.3 3.6 %convolution_convert_fusion.1 = bf16[512,1024]{1,0:T(8,128)(2,1)} fusion(bf16[512,1024]{1,0:T(8,128)(2,1)S(1)} %copy-done, bf16[512,1024]{1,0:T(8,128)(2,1)} %all-gather.2.cloned.1.call-done, bf16[1024,512]{1,0:T(8,128)(2,1)S(1)} %copy-done.7), kind=kOutput, calls=%fused_computation.19 | convolution fusion | flops 1076625408 | bytes 4194304 | tf_op jit(solution)/shard_map/dot_general | solution.py:78
  168.9 0.0 reduce-scatter.5.cloned.1.call-update
  168.9 32.6 %reduce-scatter.5.cloned.1.call-done = bf16[512,256]{1,0:T(8,128)(2,1)} async-done(((bf16[512,1024]{1,0:T(8,128)(2,1)}), bf16[512,256]{1,0:T(8,128)(2,1)}) %reduce-scatter.5.cloned.1.call-update) | async-done | bytes 262160 | tf_op jit(solution)/shard_map/reduce_scatter | solution.py:79
  201.5 1.8 add_convert_fusion
  (15 shorter events, 0.0 us)
Async XLA Ops:
  6.5 158.8 %copy-start = (bf16[512,1024]{1,0:T(8,128)(2,1)S(1)}, bf16[512,1024]{1,0:T(8,128)(2,1)}, u32[]{:S(2)}) copy-start(bf16[512,1024]{1,0:T(8,128)(2,1)} %param.14) | copy-start | bytes 3145732
  6.5 23.1 %copy-start.2 = (bf16[512,1024]{1,0:T(8,128)(2,1)S(1)}, bf16[512,1024]{1,0:T(8,128)(2,1)}, u32[]{:S(2)}) copy-start(bf16[512,1024]{1,0:T(8,128)(2,1)} %param.8) | copy-start | bytes 3145732
  6.5 23.1 %copy-start.8 = (f32[1024]{0:T(1024)S(1)}, f32[1024]{0:T(1024)}, u32[]{:S(2)}) copy-start(f32[1024]{0:T(1024)} %param.9) | copy-start | bytes 12292
  6.5 114.5 %reduce-scatter.3.cloned.1.call-start = ((), (), s32[]{:S(2)}) async-start(), calls=%async_computation.2 | async-start | bytes 1310720 | tf_op jit(solution)/shard_map/reduce_scatter | solution.py:62
  6.5 23.1 %copy-start.6 = (bf16[3,1024,256]{2,1,0:T(8,128)(2,1)S(1)}, bf16[3,1024,256]{2,1,0:T(8,128)(2,1)}, u32[]{:S(2)}) copy-start(bf16[3,1024,256]{2,1,0:T(8,128)(2,1)} %param.10) | copy-start | bytes 4718596
  10.1 24.5 %collective-permute-start.4 = (bf16[4,128,256]{2,1,0:T(8,128)(2,1)S(1)}, bf16[4,128,256]{2,1,0:T(8,128)(2,1)}, u32[]{:S(2)}, u32[]{:S(2)}) collective-permute-start(bf16[4,128,256]{2,1,0:T(8,128)(2,1)S(1)} %bitcast.30), channel_id=1, source_target_pairs={{0,8},{4,12},{8,16},{12,20},{16,24},{20,28},{24,32},{28,36},{32,40... | collective-permute-start | bytes 786440 | tf_op jit(solution)/shard_map/ppermute | solution.py:15
  13.6 24.6 %collective-permute-start.5 = (bf16[4,128,256]{2,1,0:T(8,128)(2,1)S(1)}, bf16[4,128,256]{2,1,0:T(8,128)(2,1)}, u32[]{:S(2)}, u32[]{:S(2)}) collective-permute-start(bf16[4,128,256]{2,1,0:T(8,128)(2,1)S(1)} %bitcast.31), channel_id=1, source_target_pairs={{0,4},{4,8},{8,12},{12,16},{16,20},{20,24},{24,28},{28,32},{32,36}... | collective-permute-start | bytes 786440 | tf_op jit(solution)/shard_map/ppermute | solution.py:15
  15.5 28.7 %collective-permute-start.6 = (bf16[4,128,256]{2,1,0:T(8,128)(2,1)S(1)}, bf16[4,128,256]{2,1,0:T(8,128)(2,1)S(1)}, u32[]{:S(2)}, u32[]{:S(2)}) collective-permute-start(bf16[4,128,256]{2,1,0:T(8,128)(2,1)S(1)} %bitcast.32), channel_id=1, source_target_pairs={{0,508},{4,0},{8,4},{12,8},{16,12},{20,16},{24,20},{28,24},{32,28}... | collective-permute-start | bytes 786440 | tf_op jit(solution)/shard_map/ppermute | solution.py:15
  19.2 33.3 %collective-permute-start.7 = (bf16[4,128,256]{2,1,0:T(8,128)(2,1)S(1)}, bf16[4,128,256]{2,1,0:T(8,128)(2,1)S(1)}, u32[]{:S(2)}, u32[]{:S(2)}) collective-permute-start(bf16[4,128,256]{2,1,0:T(8,128)(2,1)S(1)} %bitcast.33), channel_id=1, source_target_pairs={{0,504},{4,508},{8,0},{12,4},{16,8},{20,12},{24,16},{28,20},{32,24... | collective-permute-start | bytes 786440 | tf_op jit(solution)/shard_map/ppermute | solution.py:15
  30.1 35.1 %collective-permute-start = (bf16[4,128,256]{2,1,0:T(8,128)(2,1)S(1)}, bf16[4,128,256]{2,1,0:T(8,128)(2,1)}, u32[]{:S(2)}, u32[]{:S(2)}) collective-permute-start(bf16[4,128,256]{2,1,0:T(8,128)(2,1)S(1)} %bitcast.25), channel_id=1, source_target_pairs={{0,8},{4,12},{8,16},{12,20},{16,24},{20,28},{24,32},{28,36},{32,40... | collective-permute-start | bytes 786440 | tf_op jit(solution)/shard_map/ppermute | solution.py:15
  34.6 32.4 %collective-permute-start.1 = (bf16[4,128,256]{2,1,0:T(8,128)(2,1)S(1)}, bf16[4,128,256]{2,1,0:T(8,128)(2,1)}, u32[]{:S(2)}, u32[]{:S(2)}) collective-permute-start(bf16[4,128,256]{2,1,0:T(8,128)(2,1)S(1)} %bitcast.26), channel_id=1, source_target_pairs={{0,4},{4,8},{8,12},{12,16},{16,20},{20,24},{24,28},{28,32},{32,36}... | collective-permute-start | bytes 786440 | tf_op jit(solution)/shard_map/ppermute | solution.py:15
  38.2 31.2 %collective-permute-start.2 = (bf16[4,128,256]{2,1,0:T(8,128)(2,1)S(1)}, bf16[4,128,256]{2,1,0:T(8,128)(2,1)}, u32[]{:S(2)}, u32[]{:S(2)}) collective-permute-start(bf16[4,128,256]{2,1,0:T(8,128)(2,1)S(1)} %bitcast.27), channel_id=1, source_target_pairs={{0,508},{4,0},{8,4},{12,8},{16,12},{20,16},{24,20},{28,24},{32,28}... | collective-permute-start | bytes 786440 | tf_op jit(solution)/shard_map/ppermute | solution.py:15
  44.2 26.9 %collective-permute-start.3 = (bf16[4,128,256]{2,1,0:T(8,128)(2,1)S(1)}, bf16[4,128,256]{2,1,0:T(8,128)(2,1)}, u32[]{:S(2)}, u32[]{:S(2)}) collective-permute-start(bf16[4,128,256]{2,1,0:T(8,128)(2,1)S(1)} %bitcast.28), channel_id=1, source_target_pairs={{0,504},{4,508},{8,0},{12,4},{16,8},{20,12},{24,16},{28,20},{32,24... | collective-permute-start | bytes 786440 | tf_op jit(solution)/shard_map/ppermute | solution.py:15
  62.0 3.2 %copy-start.1 = (f32[4,4,128,1024]{3,2,1,0:T(8,128)}, f32[4,4,128,1024]{3,2,1,0:T(8,128)S(1)}, u32[]{:S(2)}) copy-start(f32[4,4,128,1024]{3,2,1,0:T(8,128)S(1)} %fusion.4) | copy-start | bytes 25165828
  78.0 12.4 %copy-start.5 = (bf16[256,1024]{1,0:T(8,128)(2,1)S(1)}, bf16[256,1024]{1,0:T(8,128)(2,1)}, u32[]{:S(2)}) copy-start(bf16[256,1024]{1,0:T(8,128)(2,1)} %param.11) | copy-start | bytes 1572868
  90.1 30.9 %copy-start.3 = (bf16[512,1024]{1,0:T(8,128)(2,1)S(1)}, bf16[512,1024]{1,0:T(8,128)(2,1)}, u32[]{:S(2)}) copy-start(bf16[512,1024]{1,0:T(8,128)(2,1)} %param.8) | copy-start | bytes 3145732
  91.8 73.5 %copy-start.7 = (bf16[1024,512]{1,0:T(8,128)(2,1)S(1)}, bf16[1024,512]{1,0:T(8,128)(2,1)}, u32[]{:S(2)}) copy-start(bf16[1024,512]{1,0:T(8,128)(2,1)} %param.13) | copy-start | bytes 3145732
  91.8 73.5 %all-gather.2.cloned.1.call-start = ((), (), s32[]{:S(2)}) async-start(), calls=%async_computation.3 | async-start | bytes 1310720 | tf_op jit(solution)/shard_map/all_gather | solution.py:74
  132.4 69.1 %copy-start.4 = (bf16[512,256]{1,0:T(8,128)(2,1)S(1)}, bf16[512,256]{1,0:T(8,128)(2,1)}, u32[]{:S(2)}) copy-start(bf16[512,256]{1,0:T(8,128)(2,1)} %reduce-scatter.3.cloned.1.call-done) | copy-start | bytes 786436
  132.4 69.1 %reduce-scatter.5.cloned.1.call-start = ((), (), s32[]{:S(2)}) async-start(), calls=%async_computation.4 | async-start | bytes 1310720 | tf_op jit(solution)/shard_map/reduce_scatter | solution.py:79
Sparse Core Ops, SparseCore 0:
  92.0 29.0 reduce-scatter.2
  132.5 32.8 all-gather.1
  169.1 32.3 reduce-scatter.4
where the time goes:
time: 211 us; the launch traced here: 210 us
  waiting for transfers between devices  93.9 us (45%)
  starting transfers between devices  34.6 us (16%)
  local copies, waits for them, and re-layouts  26.8 us (13%)
  matrix products  23.6 us (11%)
  between operations  13.3 us (6%)
  other arithmetic  9.3 us (4%)
  blocking collectives  8.37 us (4%)
    ppermute x8, starting transfers between devices, from_behind(): lax.ppermute(array, axis, [(i, (i + by) % length) for i in range(length)])  34.5 us
    all_gather x1, waiting for transfers between devices, per_device(): normed2 = lax.all_gather(normed_cols, 'mp', axis=1, tiled=True)  32.9 us
    reduce_scatter x1, waiting for transfers between devices, per_device(): lax.psum_scatter(down_term.astype(jnp.bfloat16), 'mp', scatter_dimension=...  32.6 us
    reduce_scatter x1, waiting for transfers between devices, per_device(): lax.psum_scatter(partial_value.astype(jnp.bfloat16), 'mp', scatter_dimens...  28.3 us
    dot_general x1, matrix products, per_device(): jnp.einsum('phqk,pkhd->pqhd', probs, vals_nb, preferred_element_type=jnp....  12.1 us
    unnamed x26, local copies, waits for them, and re-layouts  11.6 us
    psum x1, blocking collectives, per_device(): square_sum = lax.psum(jnp.sum(residual_cols * residual_cols, axis=1), 'mp')  8.37 us
  transfers between devices with their start and end apart: 11, of which 3 were waited for; matrix products, arithmetic and copies ran while one was open for 12% of the time, Pallas kernels for 0%

commit v1 on v0

--- a/solution.py
+++ b/solution.py
@@ -71,7 +71,9 @@
     square_sum = lax.psum(jnp.sum(residual_cols * residual_cols, axis=1), "mp")
     inverse_rms = lax.rsqrt(square_sum / D + 1e-05)
     normed_cols = (residual_cols * inverse_rms[:, None] * gain_cols).astype(jnp.bfloat16)
-    normed2 = lax.all_gather(normed_cols, "mp", axis=1, tiled=True)
+    normed2 = jnp.concatenate(
+        lax.all_to_all(jnp.stack([normed_cols] * lax.axis_size("mp")), "mp", 0, 0), axis=1
+    )
     hidden = jax.nn.gelu(
         jnp.dot(normed2, w_up, preferred_element_type=jnp.float32), approximate=True
     ).astype(jnp.bfloat16)

time: 211 us -> 191 us (0.905)
  the two profiles are of different devices: /device:TPU:8 before, /device:TPU:16 now
where the time goes in v1:
time: 191 us; the launch traced here: 190 us
  waiting for transfers between devices  64.7 us (34%)
  starting transfers between devices  29.4 us (15%)
  local copies, waits for them, and re-layouts  27 us (14%)
  matrix products  23.7 us (12%)
  blocking collectives  22.8 us (12%)
  between operations  13.6 us (7%)
  other arithmetic  8.59 us (4%)
    reduce_scatter x1, waiting for transfers between devices, per_device(): lax.psum_scatter(partial_value.astype(jnp.bfloat16), 'mp', scatter_dimens...  33.5 us
    reduce_scatter x1, waiting for transfers between devices, per_device(): lax.psum_scatter(down_term.astype(jnp.bfloat16), 'mp', scatter_dimension=...  31.1 us
    ppermute x8, starting transfers between devices, from_behind(): lax.ppermute(array, axis, [(i, (i + by) % length) for i in range(length)])  29.3 us
    all_to_all x1, blocking collectives, per_device(): lax.all_to_all(jnp.stack([normed_cols] * lax.axis_size('mp')), 'mp', 0, 0)  14.6 us
    dot_general x1, matrix products, per_device(): jnp.einsum('phqk,pkhd->pqhd', probs, vals_nb, preferred_element_type=jnp....  12.1 us
    unnamed x24, local copies, waits for them, and re-layouts  11.6 us
    psum x1, blocking collectives, per_device(): square_sum = lax.psum(jnp.sum(residual_cols * residual_cols, axis=1), 'mp')  8.24 us
  transfers between devices with their start and end apart: 10, of which 2 were waited for; matrix products, arithmetic and copies ran while one was open for 14% of the time, Pallas kernels for 0%

profile of v1, /device:TPU:16, one launch (start us, length us, event | category | flops | bytes accessed | tf_op | source)
XLA Modules:
  0.0 189.8 jit_solution(2145495423289908021)
XLA Ops:
  6.5 0.0 copy-start
  6.5 0.0 copy-start.6
  6.6 1.7 fusion.9
  8.2 1.9 convolution_convert_fusion.2
  10.1 3.2 %collective-permute-start.4 = (bf16[4,128,256]{2,1,0:T(8,128)(2,1)S(1)}, bf16[4,128,256]{2,1,0:T(8,128)(2,1)}, u32[]{:S(2)}, u32[]{:S(2)}) collective-permute-start(bf16[4,128,256]{2,1,0:T(8,128)(2,1)S(1)} %bitcast.34), channel_id=1, source_target_pairs={{0,8},{4,12},{8,16},{12,20},{16,24},{20,28},{24,32},{28,36},{32,40... | collective-permute-start | bytes 786440 | tf_op jit(solution)/shard_map/ppermute | solution.py:15
  13.3 1.9 %collective-permute-start.5 = (bf16[4,128,256]{2,1,0:T(8,128)(2,1)S(1)}, bf16[4,128,256]{2,1,0:T(8,128)(2,1)}, u32[]{:S(2)}, u32[]{:S(2)}) collective-permute-start(bf16[4,128,256]{2,1,0:T(8,128)(2,1)S(1)} %bitcast.35), channel_id=1, source_target_pairs={{0,4},{4,8},{8,12},{12,16},{16,20},{20,24},{24,28},{28,32},{32,36}... | collective-permute-start | bytes 786440 | tf_op jit(solution)/shard_map/ppermute | solution.py:15
  15.2 3.6 %collective-permute-start.6 = (bf16[4,128,256]{2,1,0:T(8,128)(2,1)S(1)}, bf16[4,128,256]{2,1,0:T(8,128)(2,1)S(1)}, u32[]{:S(2)}, u32[]{:S(2)}) collective-permute-start(bf16[4,128,256]{2,1,0:T(8,128)(2,1)S(1)} %bitcast.36), channel_id=1, source_target_pairs={{0,508},{4,0},{8,4},{12,8},{16,12},{20,16},{24,20},{28,24},{32,28}... | collective-permute-start | bytes 786440 | tf_op jit(solution)/shard_map/ppermute | solution.py:15
  18.9 2.7 %collective-permute-start.7 = (bf16[4,128,256]{2,1,0:T(8,128)(2,1)S(1)}, bf16[4,128,256]{2,1,0:T(8,128)(2,1)S(1)}, u32[]{:S(2)}, u32[]{:S(2)}) collective-permute-start(bf16[4,128,256]{2,1,0:T(8,128)(2,1)S(1)} %bitcast.37), channel_id=1, source_target_pairs={{0,504},{4,508},{8,0},{12,4},{16,8},{20,12},{24,16},{28,20},{32,24... | collective-permute-start | bytes 786440 | tf_op jit(solution)/shard_map/ppermute | solution.py:15
  21.5 0.0 copy-done.2
  21.5 0.0 copy-done.7
  21.6 0.0 copy-done.6
  21.6 0.5 convolution_convert_fusion.4
  22.1 3.2 %collective-permute-start = (bf16[4,128,256]{2,1,0:T(8,128)(2,1)S(1)}, bf16[4,128,256]{2,1,0:T(8,128)(2,1)}, u32[]{:S(2)}, u32[]{:S(2)}) collective-permute-start(bf16[4,128,256]{2,1,0:T(8,128)(2,1)S(1)} %bitcast.29), channel_id=1, source_target_pairs={{0,8},{4,12},{8,16},{12,20},{16,24},{20,28},{24,32},{28,36},{32,40... | collective-permute-start | bytes 786440 | tf_op jit(solution)/shard_map/ppermute | solution.py:15
  25.3 0.5 convolution_convert_fusion.3
  25.8 0.8 compare_select_fusion
  26.6 0.1 copy.18
  26.6 0.1 reshape.49
  26.7 1.0 reshape.70
  27.8 0.0 collective-permute-done.4
  27.8 1.9 %collective-permute-start.1 = (bf16[4,128,256]{2,1,0:T(8,128)(2,1)S(1)}, bf16[4,128,256]{2,1,0:T(8,128)(2,1)}, u32[]{:S(2)}, u32[]{:S(2)}) collective-permute-start(bf16[4,128,256]{2,1,0:T(8,128)(2,1)S(1)} %bitcast.30), channel_id=1, source_target_pairs={{0,4},{4,8},{8,12},{12,16},{16,20},{20,24},{24,28},{28,32},{32,36}... | collective-permute-start | bytes 786440 | tf_op jit(solution)/shard_map/ppermute | solution.py:15
  29.7 1.7 constant_dynamic-update-slice_fusion.9
  31.4 0.0 collective-permute-done.5
  31.4 3.6 %collective-permute-start.2 = (bf16[4,128,256]{2,1,0:T(8,128)(2,1)S(1)}, bf16[4,128,256]{2,1,0:T(8,128)(2,1)}, u32[]{:S(2)}, u32[]{:S(2)}) collective-permute-start(bf16[4,128,256]{2,1,0:T(8,128)(2,1)S(1)} %bitcast.31), channel_id=1, source_target_pairs={{0,508},{4,0},{8,4},{12,8},{16,12},{20,16},{24,20},{28,24},{32,28}... | collective-permute-start | bytes 786440 | tf_op jit(solution)/shard_map/ppermute | solution.py:15
  35.0 1.7 constant_dynamic-update-slice_fusion.8
  36.7 0.7 constant_dynamic-update-slice_fusion.7
  37.4 0.0 collective-permute-done.6
  37.4 9.2 %collective-permute-start.3 = (bf16[4,128,256]{2,1,0:T(8,128)(2,1)S(1)}, bf16[4,128,256]{2,1,0:T(8,128)(2,1)}, u32[]{:S(2)}, u32[]{:S(2)}) collective-permute-start(bf16[4,128,256]{2,1,0:T(8,128)(2,1)S(1)} %bitcast.32), channel_id=1, source_target_pairs={{0,504},{4,508},{8,0},{12,4},{16,8},{20,12},{24,16},{28,20},{32,24... | collective-permute-start | bytes 786440 | tf_op jit(solution)/shard_map/ppermute | solution.py:15
  46.6 0.7 constant_dynamic-update-slice_fusion.6
  47.3 0.0 collective-permute-done.7
  47.3 0.7 constant_dynamic-update-slice_fusion.5
  48.0 2.0 %gather_fusion.1 = bf16[32,128,256]{2,1,0:T(8,128)(2,1)S(1)} fusion(bf16[20,128,256]{2,1,0:T(8,128)(2,1)} %constant_dynamic-update-slice_fusion.5, s32[1024]{0:T(1024)S(1)} %pad_clamp_fusion), kind=kCustom, calls=%fused_computation.1 | custom fusion | bytes 4194432 | tf_op jit(solution)/shard_map/gather | solution.py:52
  50.0 3.3 %reshape.71 = bf16[4,1024,4,64]{3,2,1,0:T(4,128)(2,1)} reshape(bf16[32,128,256]{2,1,0:T(8,128)(2,1)S(1)} %gather_fusion.1) | data formatting | bytes 4194304 | tf_op jit(solution)/shard_map/reshape | solution.py:52
  53.3 3.6 %fusion.4 = f32[4,4,128,1024]{3,2,1,0:T(8,128)S(1)} fusion(bf16[4,1024,4,64]{3,2,1,0:T(4,128)(2,1)} %reshape.71, bf16[4,128,4,64]{3,2,1,0:T(4,128)(2,1)} %reshape.70), kind=kOutput, calls=%fused_computation.7 | convolution fusion | flops 268435456 | bytes 10747904 | tf_op jit(solution)/shard_map/pqhd,pkhd->phqk/dot_general | solution.py:55
  56.9 2.2 %fusion.62 = f32[4,4,128]{2,1,0:T(4,128)S(1)} fusion(f32[4,4,128,1024]{3,2,1,0:T(8,128)S(1)} %fusion.4), kind=kOutput, calls=%fused_computation.87 | output fusion | flops 8389631 | bytes 8396800 | tf_op jit(solution)/shard_map/sub | solution.py:58
  59.1 1.0 copy-done.1
  60.2 0.0 collective-permute-done
  60.2 1.7 constant_dynamic-update-slice_fusion.4
  61.8 0.0 collective-permute-done.1
  61.8 1.7 constant_dynamic-update-slice_fusion.3
  63.5 0.7 constant_dynamic-update-slice_fusion.2
  64.2 0.0 collective-permute-done.2
  64.3 1.7 constant_dynamic-update-slice_fusion.1
  65.9 0.0 collective-permute-done.3
  65.9 1.7 constant_dynamic-update-slice_fusion
  67.6 2.0 %gather_fusion = bf16[32,128,256]{2,1,0:T(8,128)(2,1)S(1)} fusion(bf16[20,128,256]{2,1,0:T(8,128)(2,1)} %constant_dynamic-update-slice_fusion, s32[1024]{0:T(1024)S(1)} %pad_clamp_fusion), kind=kCustom, calls=%fused_computation | custom fusion | bytes 4194432 | tf_op jit(solution)/shard_map/gather | solution.py:53
  69.6 3.3 %reshape.69 = bf16[4,1024,4,64]{3,2,1,0:T(4,128)(2,1)} reshape(bf16[32,128,256]{2,1,0:T(8,128)(2,1)S(1)} %gather_fusion) | data formatting | bytes 4194304 | tf_op jit(solution)/shard_map/reshape | solution.py:53
  72.9 12.1 %fusion.15 = bf16[4,128,4,64]{1,3,2,0:T(8,128)(2,1)S(1)} fusion(f32[4,4,128]{2,1,0:T(4,128)S(1)} %fusion.62, bf16[4,1024,4,64]{3,2,1,0:T(4,128)(2,1)} %reshape.69, f32[4,4,128,1024]{3,2,1,0:T(8,128)} %copy-done.1), kind=kOutput, calls=%fused_computation.24 | convolution fusion | flops 279055360 | bytes 10756096 | tf_op jit(solution)/shard_map/phqk,pkhd->pqhd/dot_general | solution.py:59
  85.0 0.0 copy-start.3
  85.1 0.2 copy.25
  85.3 1.5 convolution_convert_fusion
  86.7 0.0 reduce-scatter.3.cloned.1.call-update
  86.8 0.0 reduce-scatter.5.cloned.1.call-start
  86.8 0.8 dynamic_slice.11
  87.6 33.5 %reduce-scatter.3.cloned.1.call-done = bf16[512,256]{1,0:T(8,128)(2,1)} async-done(((bf16[512,1024]{1,0:T(8,128)(2,1)}), bf16[512,256]{1,0:T(8,128)(2,1)}) %reduce-scatter.3.cloned.1.call-update) | async-done | bytes 262160 | tf_op jit(solution)/shard_map/reduce_scatter | solution.py:62
  121.1 1.1 multiply_reduce_fusion.1
  122.2 8.2 %psum.7 = f32[512]{0:T(512)S(1)} all-reduce(f32[512]{0:T(512)S(1)} %multiply_reduce_fusion.1), channel_id=1, replica_groups=mesh['patch'=128,'mp'=4] {'mp'}, use_global_device_ids=true, to_apply=%region_5.6 | all-reduce | flops 512 | bytes 4096 | tf_op jit(solution)/shard_map/psum | solution.py:71
  130.5 1.1 multiply_convert_fusion
  131.6 0.1 copy.26
  131.7 0.1 stack.2
  131.8 14.6 %all_to_all.5 = bf16[4,512,256]{1,2,0:T(8,128)(2,1)S(1)} all-to-all(bf16[4,512,256]{1,2,0:T(8,128)(2,1)S(1)} %stack.2), channel_id=1, replica_groups=mesh['patch'=128,'mp'=4] {'mp'}, dimensions={0} | all-to-all | bytes 2097152 | tf_op jit(solution)/shard_map/all_to_all | solution.py:75
  146.4 3.7 %convolution_convert_fusion.1 = bf16[512,1024]{1,0:T(8,128)(2,1)} fusion(bf16[512,1024]{1,0:T(8,128)(2,1)S(1)} %copy-done, bf16[512,1024]{0,1:T(8,128)(2,1)S(1)} %bitcast.28, bf16[1024,512]{1,0:T(8,128)(2,1)} %param.13), kind=kOutput, calls=%fused_computation.19 | convolution fusion | flops 1076625408 | bytes 4194304 | tf_op jit(solution)/shard_map/dot_general | solution.py:80
  150.1 0.0 reduce-scatter.5.cloned.1.call-update
  150.1 31.1 %reduce-scatter.5.cloned.1.call-done = bf16[512,256]{1,0:T(8,128)(2,1)} async-done(((bf16[512,1024]{1,0:T(8,128)(2,1)}), bf16[512,256]{1,0:T(8,128)(2,1)}) %reduce-scatter.5.cloned.1.call-update) | async-done | bytes 262160 | tf_op jit(solution)/shard_map/reduce_scatter | solution.py:81
  181.2 1.8 add_convert_fusion
  (13 shorter events, 0.0 us)
Async XLA Ops:
  6.5 139.9 %copy-start = (bf16[512,1024]{1,0:T(8,128)(2,1)S(1)}, bf16[512,1024]{1,0:T(8,128)(2,1)}, u32[]{:S(2)}) copy-start(bf16[512,1024]{1,0:T(8,128)(2,1)} %param.14) | copy-start | bytes 3145732
  6.5 15.0 %copy-start.2 = (bf16[512,1024]{1,0:T(8,128)(2,1)S(1)}, bf16[512,1024]{1,0:T(8,128)(2,1)}, u32[]{:S(2)}) copy-start(bf16[512,1024]{1,0:T(8,128)(2,1)} %param.8) | copy-start | bytes 3145732
  6.5 15.0 %copy-start.7 = (f32[1024]{0:T(1024)S(1)}, f32[1024]{0:T(1024)}, u32[]{:S(2)}) copy-start(f32[1024]{0:T(1024)} %param.9) | copy-start | bytes 12292
  6.5 114.6 %reduce-scatter.3.cloned.1.call-start = ((), (), s32[]{:S(2)}) async-start(), calls=%async_computation.3 | async-start | bytes 1310720 | tf_op jit(solution)/shard_map/reduce_scatter | solution.py:62
  6.5 15.0 %copy-start.6 = (bf16[3,1024,256]{2,1,0:T(8,128)(2,1)S(1)}, bf16[3,1024,256]{2,1,0:T(8,128)(2,1)}, u32[]{:S(2)}) copy-start(bf16[3,1024,256]{2,1,0:T(8,128)(2,1)} %param.10) | copy-start | bytes 4718596
  10.1 17.7 %collective-permute-start.4 = (bf16[4,128,256]{2,1,0:T(8,128)(2,1)S(1)}, bf16[4,128,256]{2,1,0:T(8,128)(2,1)}, u32[]{:S(2)}, u32[]{:S(2)}) collective-permute-start(bf16[4,128,256]{2,1,0:T(8,128)(2,1)S(1)} %bitcast.34), channel_id=1, source_target_pairs={{0,8},{4,12},{8,16},{12,20},{16,24},{20,28},{24,32},{28,36},{32,40... | collective-permute-start | bytes 786440 | tf_op jit(solution)/shard_map/ppermute | solution.py:15
  13.3 18.1 %collective-permute-start.5 = (bf16[4,128,256]{2,1,0:T(8,128)(2,1)S(1)}, bf16[4,128,256]{2,1,0:T(8,128)(2,1)}, u32[]{:S(2)}, u32[]{:S(2)}) collective-permute-start(bf16[4,128,256]{2,1,0:T(8,128)(2,1)S(1)} %bitcast.35), channel_id=1, source_target_pairs={{0,4},{4,8},{8,12},{12,16},{16,20},{20,24},{24,28},{28,32},{32,36}... | collective-permute-start | bytes 786440 | tf_op jit(solution)/shard_map/ppermute | solution.py:15
  15.2 22.2 %collective-permute-start.6 = (bf16[4,128,256]{2,1,0:T(8,128)(2,1)S(1)}, bf16[4,128,256]{2,1,0:T(8,128)(2,1)S(1)}, u32[]{:S(2)}, u32[]{:S(2)}) collective-permute-start(bf16[4,128,256]{2,1,0:T(8,128)(2,1)S(1)} %bitcast.36), channel_id=1, source_target_pairs={{0,508},{4,0},{8,4},{12,8},{16,12},{20,16},{24,20},{28,24},{32,28}... | collective-permute-start | bytes 786440 | tf_op jit(solution)/shard_map/ppermute | solution.py:15
  18.9 28.4 %collective-permute-start.7 = (bf16[4,128,256]{2,1,0:T(8,128)(2,1)S(1)}, bf16[4,128,256]{2,1,0:T(8,128)(2,1)S(1)}, u32[]{:S(2)}, u32[]{:S(2)}) collective-permute-start(bf16[4,128,256]{2,1,0:T(8,128)(2,1)S(1)} %bitcast.37), channel_id=1, source_target_pairs={{0,504},{4,508},{8,0},{12,4},{16,8},{20,12},{24,16},{28,20},{32,24... | collective-permute-start | bytes 786440 | tf_op jit(solution)/shard_map/ppermute | solution.py:15
  22.1 38.1 %collective-permute-start = (bf16[4,128,256]{2,1,0:T(8,128)(2,1)S(1)}, bf16[4,128,256]{2,1,0:T(8,128)(2,1)}, u32[]{:S(2)}, u32[]{:S(2)}) collective-permute-start(bf16[4,128,256]{2,1,0:T(8,128)(2,1)S(1)} %bitcast.29), channel_id=1, source_target_pairs={{0,8},{4,12},{8,16},{12,20},{16,24},{20,28},{24,32},{28,36},{32,40... | collective-permute-start | bytes 786440 | tf_op jit(solution)/shard_map/ppermute | solution.py:15
  27.8 34.0 %collective-permute-start.1 = (bf16[4,128,256]{2,1,0:T(8,128)(2,1)S(1)}, bf16[4,128,256]{2,1,0:T(8,128)(2,1)}, u32[]{:S(2)}, u32[]{:S(2)}) collective-permute-start(bf16[4,128,256]{2,1,0:T(8,128)(2,1)S(1)} %bitcast.30), channel_id=1, source_target_pairs={{0,4},{4,8},{8,12},{12,16},{16,20},{20,24},{24,28},{28,32},{32,36}... | collective-permute-start | bytes 786440 | tf_op jit(solution)/shard_map/ppermute | solution.py:15
  31.4 32.9 %collective-permute-start.2 = (bf16[4,128,256]{2,1,0:T(8,128)(2,1)S(1)}, bf16[4,128,256]{2,1,0:T(8,128)(2,1)}, u32[]{:S(2)}, u32[]{:S(2)}) collective-permute-start(bf16[4,128,256]{2,1,0:T(8,128)(2,1)S(1)} %bitcast.31), channel_id=1, source_target_pairs={{0,508},{4,0},{8,4},{12,8},{16,12},{20,16},{24,20},{28,24},{32,28}... | collective-permute-start | bytes 786440 | tf_op jit(solution)/shard_map/ppermute | solution.py:15
  37.4 28.5 %collective-permute-start.3 = (bf16[4,128,256]{2,1,0:T(8,128)(2,1)S(1)}, bf16[4,128,256]{2,1,0:T(8,128)(2,1)}, u32[]{:S(2)}, u32[]{:S(2)}) collective-permute-start(bf16[4,128,256]{2,1,0:T(8,128)(2,1)S(1)} %bitcast.32), channel_id=1, source_target_pairs={{0,504},{4,508},{8,0},{12,4},{16,8},{20,12},{24,16},{28,20},{32,24... | collective-permute-start | bytes 786440 | tf_op jit(solution)/shard_map/ppermute | solution.py:15
  56.9 3.2 %copy-start.1 = (f32[4,4,128,1024]{3,2,1,0:T(8,128)}, f32[4,4,128,1024]{3,2,1,0:T(8,128)S(1)}, u32[]{:S(2)}) copy-start(f32[4,4,128,1024]{3,2,1,0:T(8,128)S(1)} %fusion.4) | copy-start | bytes 25165828
  72.9 12.4 %copy-start.5 = (bf16[256,1024]{1,0:T(8,128)(2,1)S(1)}, bf16[256,1024]{1,0:T(8,128)(2,1)}, u32[]{:S(2)}) copy-start(bf16[256,1024]{1,0:T(8,128)(2,1)} %param.11) | copy-start | bytes 1572868
  85.0 36.1 %copy-start.3 = (bf16[512,1024]{1,0:T(8,128)(2,1)S(1)}, bf16[512,1024]{1,0:T(8,128)(2,1)}, u32[]{:S(2)}) copy-start(bf16[512,1024]{1,0:T(8,128)(2,1)} %param.8) | copy-start | bytes 3145732
  86.8 94.5 %reduce-scatter.5.cloned.1.call-start = ((), (), s32[]{:S(2)}) async-start(), calls=%async_computation.4 | async-start | bytes 1310720 | tf_op jit(solution)/shard_map/reduce_scatter | solution.py:81
  146.4 34.8 %copy-start.4 = (bf16[512,256]{1,0:T(8,128)(2,1)S(1)}, bf16[512,256]{1,0:T(8,128)(2,1)}, u32[]{:S(2)}) copy-start(bf16[512,256]{1,0:T(8,128)(2,1)} %reduce-scatter.3.cloned.1.call-done) | copy-start | bytes 786436
Sparse Core Ops, SparseCore 0:
  86.9 34.1 reduce-scatter.2
  150.2 30.9 reduce-scatter.4
